TPU v7x, 256 devices: a whole 4x4x8 slice. The times are simulated.
256 devices in a mesh: tok: 32 (over z, x), head: 8 (over y, core).
Axes of the slice: x: 4, y: 4, z: 8, core: 2. Of those that a mesh axis runs over, the one named last changes fastest.
Arguments:
- embeddings: bfloat16 [4096, 4096], P('tok'), may hold values from -6 to 6
- norm_gain: bfloat16 [4096], replicated, may hold values from 0.099609375 to 1.8984375
- query_key_value_weight: bfloat16 [4096, 6144], P(None, 'head'), may hold values from -0.09375 to 0.09375
- embed_table: bfloat16 [65536, 4096], P('tok', 'head'), may hold values from -6 to 6
- rotated_cache_pages: bfloat16 [32, 32, 256, 2048], P('tok', None, None, 'head'), may hold values from -300 to 300
- page_owner_device: int32 [32, 32], P('tok'), may hold values from 0 to 31, each once within a row
- cached_length: int32 [32], P('tok'), may hold values from 2 to 8192, as said below
- vocab_shard: int32 [4096, 1], P('tok'), may hold values from 0 to 31; in each aligned block of 128 rows (0 to 127, 128 to 255, ...) at most 8 rows name the same one
- shard_row: int32 [4096], P('tok'), may hold values from 0 to 2047
- accept: int32 [4096], P('tok'), may hold values from 0 to 1, as said below
Outputs:
- out_first: bfloat16 [4096, 4096], P('tok', 'head')
- out_second: bfloat16 [4096, 4096], P('tok', 'head')
Inputs may be any that keep to these rules, and one draw needn't show every extreme that they name: `page_owner_device`: each row names every device of the tok axis once. `cached_length`: some request has exactly 8192 cached positions. `vocab_shard`: at most 8 of the 128 tokens of one request name the same shard, and some shard is named that often. `accept`: at most 32 accepted tokens in one request's block; some block has exactly 32.
All inputs are finite; a program needn't handle non-finite values.
Results may differ from a plain program's by a relative error of at most 0.017.
The roundings to bfloat16 on the way count: a program that leaves them out, or rounds other values in their place, can miss the bound.
Values may be sent and summed in bfloat16 or wider, within the bound.
No kernel may reach another device: no remote copies, remote signals or barrier semaphores. Data moves between devices by JAX's collectives and lax.ppermute only.
A program may use at most 128 MiB of HBM per device.

v0:
```python
import math
import jax
import jax.numpy as jnp
from jax import lax
from jax.sharding import PartitionSpec as P

QUERY_HEADS = 32
KEY_VALUE_HEADS = 8
HEAD_SIZE = 128
THETA = 500000.0


def angles(positions):
    steps_half = jnp.arange(HEAD_SIZE // 2, dtype=jnp.float32)
    frequency = THETA ** (-(steps_half * 2.0) / HEAD_SIZE)
    return positions.astype(jnp.float32)[:, None] * frequency[None, :]


def rotate(vectors, turning):
    half_width = vectors.shape[-1] // 2
    former = vectors[..., :half_width]
    latter = vectors[..., half_width:]
    cosine = jnp.cos(turning)
    sine_of = jnp.sin(turning)
    return jnp.concatenate(
        [former * cosine - latter * sine_of, latter * cosine + former * sine_of], axis=-1
    )


def project(inputs, norm_gain, query_key_value_weight, positions):
    widened = inputs.astype(jnp.float32)
    inverse = lax.rsqrt(jnp.mean(widened * widened, axis=-1, keepdims=True) + 1e-05)
    normed = (widened * inverse * norm_gain.astype(jnp.float32)).astype(jnp.bfloat16)
    combined = jnp.dot(normed, query_key_value_weight, preferred_element_type=jnp.float32)
    heads_per_group = QUERY_HEADS // KEY_VALUE_HEADS
    combined = combined.reshape(inputs.shape[0], -1, heads_per_group + 2, HEAD_SIZE)
    turning = angles(positions)[:, None, None, :]
    query_vectors = rotate(combined[:, :, :heads_per_group], turning).astype(jnp.bfloat16)
    block_keys = rotate(combined[:, :, heads_per_group : heads_per_group + 1], turning)[
        :, :, 0
    ].astype(jnp.bfloat16)
    block_values = combined[:, :, heads_per_group + 1].astype(jnp.bfloat16)
    return (query_vectors, block_keys, block_values)


def attend(query_vectors, block_keys, block_values, page_keys, page_values, usable):
    factor = 1.0 / math.sqrt(HEAD_SIZE)
    scores_cache = (
        jnp.einsum("bgqd,kgd->gqbk", query_vectors, page_keys, preferred_element_type=jnp.float32)
        * factor
    )
    scores_cache = jnp.where(usable[None, None, None, :], scores_cache, -1e30)
    scores_block = (
        jnp.einsum("bgqd,cgd->gqbc", query_vectors, block_keys, preferred_element_type=jnp.float32)
        * factor
    )
    highest = jnp.maximum(jnp.max(scores_cache, axis=-1), jnp.max(scores_block, axis=-1))[..., None]
    exp_cache = jnp.exp(scores_cache - highest)
    exp_block = jnp.exp(scores_block - highest)
    totals = jnp.sum(exp_cache, axis=-1) + jnp.sum(exp_block, axis=-1)
    weights_cache = exp_cache.astype(jnp.bfloat16)
    weights_block = exp_block.astype(jnp.bfloat16)
    combined = jnp.einsum(
        "gqbk,kgd->bgqd", weights_cache, page_values, preferred_element_type=jnp.float32
    )
    combined = combined + jnp.einsum(
        "gqbc,cgd->bgqd", weights_block, block_values, preferred_element_type=jnp.float32
    )
    result = combined / jnp.transpose(totals, (2, 0, 1))[..., None]
    return result.astype(jnp.bfloat16).reshape(query_vectors.shape[0], -1)


def body(
    embeddings,
    norm_gain,
    query_key_value_weight,
    embed_table,
    rotated_cache_pages,
    page_owner_device,
    cached_length,
    vocab_shard,
    shard_row,
    accept,
):
    members = lax.axis_size("tok")
    length = embeddings.shape[0]
    sources = jnp.arange(members, dtype=jnp.int32)
    positions = cached_length[0] + jnp.arange(length, dtype=jnp.int32)
    query_vectors, block_keys, block_values = project(
        embeddings, norm_gain, query_key_value_weight, positions
    )
    arrived = lax.all_to_all(rotated_cache_pages, "tok", split_axis=1, concat_axis=0, tiled=True)
    page_size = arrived.shape[2]
    arrived = arrived.reshape(members * page_size, -1, 2, HEAD_SIZE)
    page_index = jnp.sum(
        jnp.where(page_owner_device[0][:, None] == sources[None, :], sources[:, None], 0), axis=0
    )
    page_spots = page_index[:, None] * page_size + jnp.arange(page_size, dtype=jnp.int32)[None, :]
    usable = page_spots.reshape(-1) < cached_length[0]
    page_keys = arrived[:, :, 0]
    page_values = arrived[:, :, 1]

    def run_attention(query_rows, key_rows, value_rows):
        return attend(query_rows, key_rows, value_rows, page_keys, page_values, usable)

    output_one = run_attention(query_vectors, block_keys, block_values)
    target_shard = vocab_shard[:, 0]
    capacity = max(2, 2 * length // members)
    chosen = (target_shard[:, None] == sources[None, :]).astype(jnp.int32)
    earlier = (jnp.arange(length)[:, None] > jnp.arange(length)[None, :]).astype(jnp.int32)
    slot_rank = jnp.sum(jnp.dot(earlier, chosen) * chosen, axis=1)
    wanted = jnp.zeros((members, capacity), jnp.int32).at[target_shard, slot_rank].set(shard_row)
    found_rows = jnp.take(
        embed_table, lax.all_to_all(wanted, "tok", split_axis=0, concat_axis=0, tiled=True), axis=0
    )
    returned = lax.all_to_all(found_rows, "tok", split_axis=0, concat_axis=0, tiled=True)
    replacement = returned[target_shard, slot_rank]
    full_rows = lax.all_gather(replacement, "head", axis=1, tiled=True)
    replaced = jnp.where(accept[:, None] == 1, full_rows, embeddings)
    queries_two, keys_two, values_two = project(
        replaced, norm_gain, query_key_value_weight, positions
    )
    output_two = run_attention(queries_two, keys_two, values_two)
    return (output_one, output_two)


def solution(mesh):
    return jax.shard_map(
        body,
        mesh=mesh,
        in_specs=(
            P("tok", None),
            P(),
            P(None, "head"),
            P("tok", "head"),
            P("tok", None, None, "head"),
            P("tok", None),
            P("tok"),
            P("tok", None),
            P("tok"),
            P("tok"),
        ),
        out_specs=(P("tok", "head"), P("tok", "head")),
        check_vma=False,
    )
```

profile of v0, /device:TPU:12, one launch (start us, length us, event | category | flops | bytes accessed | tf_op | source)
XLA Modules:
  0.0 241.9 jit_solution(14365437352633551345)
XLA Ops:
  7.2 0.0 copy-start
  7.2 1.0 fusion.36
  8.2 0.7 fusion.89
  8.8 10.9 %scatter_fusion = s32[32,8]{0,1:T(8,128)S(1)} fusion(s32[32,8]{0,1:T(8,128)S(1)} %broadcast_in_dim.55, s32[128]{0:T(128)S(1)} %get-tuple-element.14, s32[128]{0:T(128)} %param.18), kind=kCustom, calls=%fused_computation.2 | custom fusion | bytes 2560 | tf_op jit(solution)/shard_map/scatter | solution.py:112
  19.8 0.1 copy.91
  19.9 19.1 %all_to_all.29 = s32[32,1,8]{2,1,0:T(1,128)S(1)} all-to-all(s32[32,1,8]{2,1,0:T(1,128)S(1)} %copy.91), channel_id=1, replica_groups=mesh['tok'=32,'head'=8] {'tok'}, dimensions={0} | all-to-all | bytes 2048 | tf_op jit(solution)/shard_map/all_to_all | solution.py:114
  38.9 0.1 reshape.410
  39.0 0.1 copy.92
  39.1 0.1 copy.93
  39.2 0.0 copy-done
  39.2 0.0 copy-start.6
  39.2 0.0 copy-start.7
  39.2 0.0 copy-start.8
  39.2 0.0 copy-start.3
  39.3 1.2 gather_fusion
  40.4 0.1 bitcast_select_fusion.2
  40.5 15.1 %all_to_all.30 = bf16[32,8,512]{2,1,0:T(8,128)(2,1)S(1)} all-to-all(bf16[32,8,512]{2,1,0:T(8,128)(2,1)S(1)} %bitcast_select_fusion.2), channel_id=1, replica_groups=mesh['tok'=32,'head'=8] {'tok'}, dimensions={0} | all-to-all | bytes 524288 | tf_op jit(solution)/shard_map/all_to_all | solution.py:116
  55.6 6.6 %all-to-all-start = ((bf16[1,32,256,256]{3,2,0,1:T(8,128)(2,1)}), bf16[1,32,256,256]{3,2,0,1:T(8,128)(2,1)}, u32[]{:S(2)}, u32[]{:S(2)}) async-start(bf16[1,32,256,256]{3,2,0,1:T(8,128)(2,1)} %bitcast.163), calls=%async_computation | async-start | bytes 8388608 | tf_op jit(solution)/shard_map/all_to_all | solution.py:92
  62.2 0.0 all-gather.2.cloned.1.call-start
  62.3 1.9 gather_fusion.1
  64.2 0.0 all-gather.2.cloned.1.call-update
  64.3 0.0 copy-done.6
  64.9 0.0 copy-done.7
  64.9 0.1 select_reduce_fusion
  65.0 0.1 add_compare_fusion
  65.2 0.0 copy-done.8
  65.2 0.3 multiply_cosine_fusion
  65.5 25.3 %all-gather.2.cloned.1.call-done = bf16[128,4096]{1,0:T(8,128)(2,1)} async-done(((bf16[128,512]{1,0:T(8,128)(2,1)}), bf16[128,4096]{1,0:T(8,128)(2,1)}) %all-gather.2.cloned.1.call-update) | async-done | bytes 1048592 | tf_op jit(solution)/shard_map/all_gather | solution.py:118
  90.8 0.0 copy-done.3
  90.8 1.9 fusion.17
  92.7 5.8 %fusion.41 = f32[128,768]{0,1:T(8,128)S(1)} fusion(bf16[4096,768]{1,0:T(8,128)(2,1)} %param.12, f32[128]{0:T(128)S(1)} %get-tuple-element.44, f32[4096]{0:T(1024)S(1)} %convert_element_type.83, bf16[128,4096]{1,0:T(8,128)(2,1)} %all-gather.2.cloned.1.call-done, bf16[128,4096]{1,0:T(8,128)(2,1)S(1)} %copy-done.3, pred[128]{0:T(512)(128)(4,1)S(1)} %broadcast_compare_fusion), kind=kOutput, calls=%fused_computation.48 | convolution fusion | flops 807927808 | bytes 8798848 | tf_op jit(solution)/shard_map/dot_general | solution.py:34
  98.5 0.0 copy-start.4
  98.6 0.1 copy.116
  98.7 0.1 copy.115
  98.8 5.4 %fusion.43 = f32[128,768]{0,1:T(8,128)S(1)} fusion(bf16[4096,768]{1,0:T(8,128)(2,1)} %param.12, bf16[128,4096]{1,0:T(8,128)(2,1)S(1)} %copy-done.3, f32[4096]{0:T(1024)S(1)} %convert_element_type.83, f32[128]{0:T(128)S(1)} %get-tuple-element.45), kind=kOutput, calls=%fused_computation.49 | convolution fusion | flops 807403520 | bytes 7750144 | tf_op jit(solution)/shard_map/dot_general | solution.py:34
  104.3 0.1 copy.111
  104.4 0.1 copy.112
  104.5 0.2 fusion.76
  104.8 0.1 fusion.59
  104.9 0.3 fusion.99
  105.2 0.0 copy-done.4
  105.2 0.3 fusion.101
  105.5 49.8 %all-to-all-done = bf16[1,32,256,256]{3,2,0,1:T(8,128)(2,1)} async-done(((bf16[1,32,256,256]{3,2,0,1:T(8,128)(2,1)}), bf16[1,32,256,256]{3,2,0,1:T(8,128)(2,1)}, u32[]{:S(2)}, u32[]{:S(2)}) %all-to-all-start) | async-done | bytes 4194336 | tf_op jit(solution)/shard_map/all_to_all | solution.py:92
  155.3 6.9 %reshape.435 = bf16[8192,1,2,128]{3,2,0,1:T(2,128)(2,1)} reshape(bf16[1,32,256,256]{3,2,0,1:T(8,128)(2,1)} %all-to-all-done) | data formatting | bytes 8388608 | tf_op jit(solution)/shard_map/reshape | solution.py:94
  162.3 9.8 %fusion.95 = (bf16[8192,1,1,128]{3,2,0,1:T(2,128)(2,1)S(1)}, bf16[8192,1,1,128]{3,2,0,1:T(2,128)(2,1)}) fusion(bf16[8192,1,2,128]{3,2,0,1:T(2,128)(2,1)} %reshape.435), kind=kLoop, calls=%fused_computation.135 | loop fusion | bytes 8388608 | tf_op jit(solution)/shard_map/slice | solution.py:100
  172.1 8.3 %fusion.98 = (f32[4,128]{1,0:T(4,128)}, f32[1,4,128,8192]{3,2,1,0:T(8,128)}) fusion(bf16[8192,1,1,128]{3,2,0,1:T(2,128)(2,1)S(1)} %get-tuple-element.16, bf16[128,4,64]{2,0,1:T(8,128)(2,1)S(1)} %get-tuple-element.30, bf16[128,4,64]{2,0,1:T(8,128)(2,1)S(1)} %get-tuple-element.31, pred[8192]{0:T(1024)(128)(4,1)S(1)} %lt.48), kind=kOutput, calls=%fused_computation.138 | convolution fusion | flops 1086586368 | bytes 19015680 | tf_op jit(solution)/shard_map/bgqd,kgd->gqbk/dot_general | solution.py:49
  180.3 7.7 %fusion.100 = (f32[4,128]{1,0:T(4,128)S(1)}, f32[1,4,128,8192]{3,2,1,0:T(8,128)}) fusion(bf16[8192,1,1,128]{3,2,0,1:T(2,128)(2,1)S(1)} %get-tuple-element.16, bf16[128,4,64]{2,0,1:T(8,128)(2,1)S(1)} %get-tuple-element.19, bf16[128,4,64]{2,0,1:T(8,128)(2,1)S(1)} %get-tuple-element.18, pred[8192]{0:T(1024)(128)(4,1)S(1)} %lt.48), kind=kOutput, calls=%fused_computation.140 | convolution fusion | flops 1086586368 | bytes 19015680 | tf_op jit(solution)/shard_map/bgqd,kgd->gqbk/dot_general | solution.py:49
  188.0 0.0 copy-start.5
  188.0 8.3 %copy.114 = bf16[8192,1,1,128]{0,3,2,1:T(8,128)(2,1)S(1)} copy(bf16[8192,1,1,128]{3,2,0,1:T(2,128)(2,1)} %get-tuple-element.17) | data formatting | bytes 4194304
  196.4 0.0 copy-start.2
  196.4 0.0 copy-done.5
  196.4 8.9 %fusion.2 = f32[4,128]{1,0:T(4,128)S(1)} fusion(f32[1,4,128,8192]{3,2,1,0:T(8,128)} %get-tuple-element.37, f32[4,128]{1,0:T(4,128)S(1)} %max.18), kind=kLoop, calls=%fused_computation.9 | loop fusion | flops 8388096 | bytes 16781312 | tf_op jit(solution)/shard_map/reduce_sum | solution.py:60
  205.2 0.0 copy-done.2
  205.2 8.8 %fusion.26 = f32[128,4,128]{2,0,1:T(8,128)S(1)} fusion(bf16[8192,1,1,128]{0,3,2,1:T(8,128)(2,1)S(1)} %copy.114, f32[1,4,128,8192]{3,2,1,0:T(8,128)} %get-tuple-element.37, f32[4,128]{1,0:T(4,128)S(1)} %max.18), kind=kOutput, calls=%fused_computation.40 | convolution fusion | flops 1082130432 | bytes 19138560 | tf_op jit(solution)/shard_map/gqbk,kgd->bgqd/dot_general | solution.py:63
  214.0 0.0 copy-start.1
  214.0 8.4 %fusion.31 = f32[128,4,128]{2,0,1:T(8,128)S(1)} fusion(bf16[8192,1,1,128]{0,3,2,1:T(8,128)(2,1)} %copy-done.2, f32[1,4,128,8192]{3,2,1,0:T(8,128)} %get-tuple-element.41, f32[4,128]{1,0:T(4,128)S(1)} %max.19), kind=kOutput, calls=%fused_computation.41 | convolution fusion | flops 1082130432 | bytes 19138560 | tf_op jit(solution)/shard_map/gqbk,kgd->bgqd/dot_general | solution.py:63
  222.4 8.1 %fusion.4 = f32[4,128]{1,0:T(4,128)S(1)} fusion(f32[1,4,128,8192]{3,2,1,0:T(8,128)} %get-tuple-element.41, f32[4,128]{1,0:T(4,128)S(1)} %max.19), kind=kLoop, calls=%fused_computation.11 | loop fusion | flops 8388096 | bytes 16781312 | tf_op jit(solution)/shard_map/reduce_sum | solution.py:60
  230.5 0.1 fusion.49
  230.6 0.9 fusion.38
  231.5 1.7 copy.99
  233.1 0.1 fusion.51
  233.2 1.0 fusion.40
  234.3 0.8 copy.100
  235.0 0.0 copy-done.1
  (17 shorter events, 0.1 us)
Async XLA Ops:
  7.2 32.0 %copy-start = (bf16[2048,512]{1,0:T(8,128)(2,1)S(1)}, bf16[2048,512]{1,0:T(8,128)(2,1)}, u32[]{:S(2)}) copy-start(bf16[2048,512]{1,0:T(8,128)(2,1)} %param.13) | copy-start | bytes 6291460
  39.2 25.1 %copy-start.6 = (bf16[4096]{0:T(1024)(128)(2,1)S(1)}, bf16[4096]{0:T(1024)(128)(2,1)}, u32[]{:S(2)}) copy-start(bf16[4096]{0:T(1024)(128)(2,1)} %param.11) | copy-start | bytes 24580
  39.2 25.7 %copy-start.7 = (s32[1,32]{1,0:T(1,128)S(1)}, s32[1,32]{1,0:T(1,128)}, u32[]{:S(2)}) copy-start(s32[1,32]{1,0:T(1,128)} %param.15) | copy-start | bytes 388
  39.2 25.9 %copy-start.8 = (s32[128]{0:T(128)S(1)}, s32[128]{0:T(128)}, u32[]{:S(2)}) copy-start(s32[128]{0:T(128)} %param.19) | copy-start | bytes 1540
  39.2 51.6 %copy-start.3 = (bf16[128,4096]{1,0:T(8,128)(2,1)S(1)}, bf16[128,4096]{1,0:T(8,128)(2,1)}, u32[]{:S(2)}) copy-start(bf16[128,4096]{1,0:T(8,128)(2,1)} %param.10) | copy-start | bytes 3145732
  55.6 99.7 %all-to-all-start = ((bf16[1,32,256,256]{3,2,0,1:T(8,128)(2,1)}), bf16[1,32,256,256]{3,2,0,1:T(8,128)(2,1)}, u32[]{:S(2)}, u32[]{:S(2)}) async-start(bf16[1,32,256,256]{3,2,0,1:T(8,128)(2,1)} %bitcast.163), calls=%async_computation | async-start | bytes 8388608 | tf_op jit(solution)/shard_map/all_to_all | solution.py:92
  62.2 28.6 %all-gather.2.cloned.1.call-start = ((), (), s32[]{:S(2)}) async-start(), calls=%async_computation.3 | async-start | bytes 1179648 | tf_op jit(solution)/shard_map/all_gather | solution.py:118
  98.5 6.7 %copy-start.4 = (f32[128,768]{0,1:T(8,128)}, f32[128,768]{0,1:T(8,128)S(1)}, u32[]{:S(2)}) copy-start(f32[128,768]{0,1:T(8,128)S(1)} %fusion.41) | copy-start | bytes 1179652
  188.0 8.4 %copy-start.5 = (f32[4,128]{1,0:T(4,128)S(1)}, f32[4,128]{1,0:T(4,128)}, u32[]{:S(2)}) copy-start(f32[4,128]{1,0:T(4,128)} %get-tuple-element.36) | copy-start | bytes 6148
  196.4 8.9 %copy-start.2 = (bf16[8192,1,1,128]{0,3,2,1:T(8,128)(2,1)}, bf16[8192,1,1,128]{0,3,2,1:T(8,128)(2,1)S(1)}, u32[]{:S(2)}) copy-start(bf16[8192,1,1,128]{0,3,2,1:T(8,128)(2,1)S(1)} %copy.114) | copy-start | bytes 6291460
  214.0 21.0 %copy-start.1 = (bf16[2048,512]{1,0:T(8,128)(2,1)S(1)}, bf16[2048,512]{1,0:T(8,128)(2,1)}, u32[]{:S(2)}) copy-start(bf16[2048,512]{1,0:T(8,128)(2,1)} %param.13) | copy-start | bytes 6291460
Sparse Core Ops, SparseCore 0:
  65.5 25.3 all-gather.1
where the time goes:
time: 243 us; the launch traced here: 242 us
  waiting for transfers between devices  75.2 us (31%)
  matrix products  47.7 us (20%)
  local copies, waits for them, and re-layouts  42.5 us (17%)
  blocking collectives  34.2 us (14%)
  other arithmetic  20.6 us (8%)
  between operations  15 us (6%)
  starting transfers between devices  6.66 us (3%)
    all_to_all x1, waiting for transfers between devices, body(): lax.all_to_all(rotated_cache_pages, 'tok', split_axis=1, concat_axis=0, t...  49.8 us
    all_gather x1, waiting for transfers between devices, body(): full_rows = lax.all_gather(replacement, 'head', axis=1, tiled=True)  25.3 us
    all_to_all x1, blocking collectives, body(): lax.all_to_all(wanted, 'tok', split_axis=0, concat_axis=0, tiled=True)  19.1 us
    dot_general x2, matrix products, attend(): jnp.einsum('gqbk,kgd->bgqd', weights_cache, page_values, preferred_elemen...  17.1 us
    reduce_sum x4, other arithmetic, attend(): totals = jnp.sum(exp_cache, axis=-1) + jnp.sum(exp_block, axis=-1)  17.1 us
    dot_general x2, matrix products, attend(): jnp.einsum('bgqd,kgd->gqbk', query_vectors, page_keys, preferred_element_...  15.9 us
    all_to_all x1, blocking collectives, body(): lax.all_to_all(found_rows, 'tok', split_axis=0, concat_axis=0, tiled=True)  15.1 us
    unnamed x25, local copies, waits for them, and re-layouts  11.3 us
  transfers between devices with their start and end apart: 2, of which 2 were waited for; matrix products, arithmetic and copies ran while one was open for 7% of the time, Pallas kernels for 0%

commit v1 on v0

--- a/solution.py
+++ b/solution.py
@@ -1,13 +1,31 @@
+import functools
 import math
 import jax
 import jax.numpy as jnp
 from jax import lax
 from jax.sharding import PartitionSpec as P
+from jax.lax import all_to_all, psum
 
 QUERY_HEADS = 32
 KEY_VALUE_HEADS = 8
 HEAD_SIZE = 128
 THETA = 500000.0
+
+
+def render_sizes(vector, mesh_name):
+    small = jnp.concatenate(
+        all_to_all(
+            jnp.stack([vector] * psum(1, axis_name=mesh_name), 0),
+            concat_axis=0,
+            axis_name=mesh_name,
+            split_axis=0,
+        ),
+        axis=1,
+    )
+    return small
+
+
+counts_part = functools.partial(render_sizes, mesh_name="head")
 
 
 def angles(positions):
@@ -115,7 +133,7 @@
     )
     returned = lax.all_to_all(found_rows, "tok", split_axis=0, concat_axis=0, tiled=True)
     replacement = returned[target_shard, slot_rank]
-    full_rows = lax.all_gather(replacement, "head", axis=1, tiled=True)
+    full_rows = counts_part(replacement)
     replaced = jnp.where(accept[:, None] == 1, full_rows, embeddings)
     queries_two, keys_two, values_two = project(
         replaced, norm_gain, query_key_value_weight, positions

time: 243 us -> 252 us (1.037); the launches traced: 242 us -> 247 us
  blocking collectives: 34.2 us -> 53.6 us
  between operations: 15 us -> 1.64 us
    all_to_all x1, waiting for transfers between devices: 49.8 us -> 76.4 us  [body(): lax.all_to_all(rotated_cache_pages, 'tok', split_axis=1, concat_axis=0, t...]
    all_gather x1 -> x0, waiting for transfers between devices: 25.3 us -> none  [body(): full_rows = lax.all_gather(replacement, 'head', axis=1, tiled=True)]
    all_to_all x0 -> x1, blocking collectives: none -> 19.4 us  [render_sizes(): all_to_all(jnp.stack([vector] * psum(1, axis_name=mesh_name), 0), concat_...]
    unnamed x25 -> x24, local copies, waits for them, and re-layouts: 11.3 us -> 11.1 us
  transfers between devices with their start and end apart: 2 -> 1, of which waited for: 2 -> 1; matrix products, arithmetic and copies ran while one was open for 7% -> 6% of each run, Pallas kernels for 0% -> 0%
where the time goes in v1:
time: 252 us; the launch traced here: 247 us
  waiting for transfers between devices  76.4 us (30%)
  blocking collectives  53.6 us (21%)
  matrix products  46.7 us (19%)
  local copies, waits for them, and re-layouts  42.3 us (17%)
  other arithmetic  19.4 us (8%)
  starting transfers between devices  6.64 us (3%)
    all_to_all x1, waiting for transfers between devices, body(): lax.all_to_all(rotated_cache_pages, 'tok', split_axis=1, concat_axis=0, t...  76.4 us
    all_to_all x1, blocking collectives, render_sizes(): all_to_all(jnp.stack([vector] * psum(1, axis_name=mesh_name), 0), concat_...  19.4 us
    all_to_all x1, blocking collectives, body(): lax.all_to_all(wanted, 'tok', split_axis=0, concat_axis=0, tiled=True)  19.1 us
    reduce_sum x4, other arithmetic, attend(): totals = jnp.sum(exp_cache, axis=-1) + jnp.sum(exp_block, axis=-1)  17.1 us
    dot_general x2, matrix products, attend(): jnp.einsum('gqbk,kgd->bgqd', weights_cache, page_values, preferred_elemen...  16.9 us
    dot_general x2, matrix products, attend(): jnp.einsum('bgqd,kgd->gqbk', query_vectors, page_keys, preferred_element_...  15.4 us
    all_to_all x1, blocking collectives, body(): lax.all_to_all(found_rows, 'tok', split_axis=0, concat_axis=0, tiled=True)  15.1 us
    dot_general x2, matrix products, project(): jnp.dot(normed, query_key_value_weight, preferred_element_type=jnp.float32)  11.6 us
  transfers between devices with their start and end apart: 1, of which 1 were waited for; matrix products, arithmetic and copies ran while one was open for 6% of the time, Pallas kernels for 0%

profile of v1, /device:TPU:12, one launch (start us, length us, event | category | flops | bytes accessed | tf_op | source)
XLA Modules:
  0.0 246.7 jit_solution(9440197627094265780)
XLA Ops:
  0.6 0.0 copy-start
  0.6 1.0 fusion.36
  1.6 0.7 fusion.89
  2.3 10.9 %scatter_fusion = s32[32,8]{0,1:T(8,128)S(1)} fusion(s32[32,8]{0,1:T(8,128)S(1)} %broadcast_in_dim.55, s32[128]{0:T(128)S(1)} %get-tuple-element.16, s32[128]{0:T(128)} %param.18), kind=kCustom, calls=%fused_computation.2 | custom fusion | bytes 2560 | tf_op jit(solution)/shard_map/scatter | solution.py:130
  13.3 0.1 copy.118
  13.3 19.1 %all_to_all.34 = s32[32,1,8]{2,1,0:T(1,128)S(1)} all-to-all(s32[32,1,8]{2,1,0:T(1,128)S(1)} %copy.118), channel_id=1, replica_groups=mesh['tok'=32,'head'=8] {'tok'}, dimensions={0} | all-to-all | bytes 2048 | tf_op jit(solution)/shard_map/all_to_all | solution.py:132
  32.4 0.1 reshape.420
  32.5 0.1 copy.119
  32.6 0.1 copy.120
  32.7 0.0 copy-done
  32.7 1.2 gather_fusion
  33.8 0.1 bitcast_select_fusion.3
  33.9 15.1 %all_to_all.35 = bf16[32,8,512]{2,1,0:T(8,128)(2,1)S(1)} all-to-all(bf16[32,8,512]{2,1,0:T(8,128)(2,1)S(1)} %bitcast_select_fusion.3), channel_id=1, replica_groups=mesh['tok'=32,'head'=8] {'tok'}, dimensions={0} | all-to-all | bytes 524288 | tf_op jit(solution)/shard_map/all_to_all | solution.py:134
  49.0 0.0 copy-start.3
  49.0 1.3 gather_fusion.1
  50.3 0.1 stack.2
  50.4 0.0 copy-start.5
  50.4 0.0 copy-start.6
  50.4 0.0 copy-start.7
  50.5 19.4 %all_to_all.36 = bf16[8,128,512]{2,1,0:T(8,128)(2,1)S(1)} all-to-all(bf16[8,128,512]{2,1,0:T(8,128)(2,1)S(1)} %stack.2), channel_id=1, replica_groups=mesh['tok'=32,'head'=8] {'head'}, dimensions={0} | all-to-all | bytes 2097152 | tf_op jit(solution)/shard_map/all_to_all | solution.py:17
  69.9 6.6 %all-to-all-start = ((bf16[1,32,256,256]{3,2,0,1:T(8,128)(2,1)}), bf16[1,32,256,256]{3,2,0,1:T(8,128)(2,1)}, u32[]{:S(2)}, u32[]{:S(2)}) async-start(bf16[1,32,256,256]{3,2,0,1:T(8,128)(2,1)} %bitcast.168), calls=%async_computation | async-start | bytes 8388608 | tf_op jit(solution)/shard_map/all_to_all | solution.py:110
  76.5 0.0 copy-done.3
  76.6 0.7 copy.109
  77.2 0.0 copy-done.5
  77.9 0.0 copy-done.6
  77.9 0.1 select_reduce_fusion
  78.0 0.1 add_compare_fusion
  78.1 0.0 copy-done.7
  78.2 0.3 multiply_cosine_fusion
  78.5 0.7 copy.121
  79.1 0.6 fusion.17
  79.8 5.8 %fusion.41 = f32[128,768]{0,1:T(8,128)S(1)} fusion(bf16[4096,768]{1,0:T(8,128)(2,1)} %param.12, bf16[128,4096]{0,1:T(8,128)(2,1)S(1)} %get-tuple-element.15, f32[128]{0:T(128)S(1)} %get-tuple-element.47, f32[4096]{0:T(1024)S(1)} %convert_element_type.83), kind=kOutput, calls=%fused_computation.48 | convolution fusion | flops 807403520 | bytes 7750144 | tf_op jit(solution)/shard_map/dot_general | solution.py:52
  85.6 0.1 copy.145
  85.8 0.1 copy.144
  85.9 5.8 %fusion.43 = f32[128,768]{0,1:T(8,128)S(1)} fusion(bf16[4096,768]{1,0:T(8,128)(2,1)} %param.12, bf16[128,4096]{0,1:T(8,128)(2,1)S(1)} %copy.109, f32[4096]{0:T(1024)S(1)} %convert_element_type.83, f32[128]{0:T(128)S(1)} %get-tuple-element.48), kind=kOutput, calls=%fused_computation.49 | convolution fusion | flops 807403520 | bytes 7750144 | tf_op jit(solution)/shard_map/dot_general | solution.py:52
  91.7 0.0 copy-start.4
  91.8 0.1 copy.140
  91.9 0.1 copy.141
  92.0 0.2 fusion.76
  92.3 0.1 fusion.59
  92.4 0.3 fusion.99
  92.7 0.3 fusion.101
  93.0 76.4 %all-to-all-done = bf16[1,32,256,256]{3,2,0,1:T(8,128)(2,1)} async-done(((bf16[1,32,256,256]{3,2,0,1:T(8,128)(2,1)}), bf16[1,32,256,256]{3,2,0,1:T(8,128)(2,1)}, u32[]{:S(2)}, u32[]{:S(2)}) %all-to-all-start) | async-done | bytes 4194336 | tf_op jit(solution)/shard_map/all_to_all | solution.py:110
  169.4 6.9 %reshape.445 = bf16[8192,1,2,128]{3,2,0,1:T(2,128)(2,1)} reshape(bf16[1,32,256,256]{3,2,0,1:T(8,128)(2,1)} %all-to-all-done) | data formatting | bytes 8388608 | tf_op jit(solution)/shard_map/reshape | solution.py:112
  176.3 0.0 copy-done.4
  176.3 9.8 %fusion.95 = (bf16[8192,1,1,128]{3,2,0,1:T(2,128)(2,1)S(1)}, bf16[8192,1,1,128]{3,2,0,1:T(2,128)(2,1)}) fusion(bf16[8192,1,2,128]{3,2,0,1:T(2,128)(2,1)} %reshape.445), kind=kLoop, calls=%fused_computation.135 | loop fusion | bytes 8388608 | tf_op jit(solution)/shard_map/slice | solution.py:118
  186.1 7.7 %fusion.98 = (f32[4,128]{1,0:T(4,128)S(1)}, f32[1,4,128,8192]{3,2,1,0:T(8,128)}) fusion(bf16[8192,1,1,128]{3,2,0,1:T(2,128)(2,1)S(1)} %get-tuple-element.18, bf16[128,4,64]{2,0,1:T(8,128)(2,1)S(1)} %get-tuple-element.33, bf16[128,4,64]{2,0,1:T(8,128)(2,1)S(1)} %get-tuple-element.34, pred[8192]{0:T(1024)(128)(4,1)S(1)} %lt.48), kind=kOutput, calls=%fused_computation.138 | convolution fusion | flops 1086586368 | bytes 19015680 | tf_op jit(solution)/shard_map/bgqd,kgd->gqbk/dot_general | solution.py:67
  193.8 7.7 %fusion.100 = (f32[4,128]{1,0:T(4,128)S(1)}, f32[1,4,128,8192]{3,2,1,0:T(8,128)}) fusion(bf16[8192,1,1,128]{3,2,0,1:T(2,128)(2,1)S(1)} %get-tuple-element.18, bf16[128,4,64]{2,0,1:T(8,128)(2,1)S(1)} %get-tuple-element.22, bf16[128,4,64]{2,0,1:T(8,128)(2,1)S(1)} %get-tuple-element.21, pred[8192]{0:T(1024)(128)(4,1)S(1)} %lt.48), kind=kOutput, calls=%fused_computation.140 | convolution fusion | flops 1086586368 | bytes 19015680 | tf_op jit(solution)/shard_map/bgqd,kgd->gqbk/dot_general | solution.py:67
  201.5 8.3 %copy.143 = bf16[8192,1,1,128]{0,3,2,1:T(8,128)(2,1)S(1)} copy(bf16[8192,1,1,128]{3,2,0,1:T(2,128)(2,1)} %get-tuple-element.19) | data formatting | bytes 4194304
  209.8 0.0 copy-start.2
  209.8 8.9 %fusion.2 = f32[4,128]{1,0:T(4,128)S(1)} fusion(f32[1,4,128,8192]{3,2,1,0:T(8,128)} %get-tuple-element.40, f32[4,128]{1,0:T(4,128)S(1)} %max.18), kind=kLoop, calls=%fused_computation.9 | loop fusion | flops 8388096 | bytes 16781312 | tf_op jit(solution)/shard_map/reduce_sum | solution.py:78
  218.7 0.0 copy-done.2
  218.7 8.8 %fusion.26 = f32[128,4,128]{2,0,1:T(8,128)S(1)} fusion(bf16[8192,1,1,128]{0,3,2,1:T(8,128)(2,1)S(1)} %copy.143, f32[1,4,128,8192]{3,2,1,0:T(8,128)} %get-tuple-element.40, f32[4,128]{1,0:T(4,128)S(1)} %max.18), kind=kOutput, calls=%fused_computation.40 | convolution fusion | flops 1082130432 | bytes 19138560 | tf_op jit(solution)/shard_map/gqbk,kgd->bgqd/dot_general | solution.py:81
  227.5 0.0 copy-start.1
  227.5 8.2 %fusion.31 = f32[128,4,128]{2,0,1:T(8,128)S(1)} fusion(bf16[8192,1,1,128]{0,3,2,1:T(8,128)(2,1)} %copy-done.2, f32[1,4,128,8192]{3,2,1,0:T(8,128)} %get-tuple-element.44, f32[4,128]{1,0:T(4,128)S(1)} %max.19), kind=kOutput, calls=%fused_computation.41 | convolution fusion | flops 1082130432 | bytes 19138560 | tf_op jit(solution)/shard_map/gqbk,kgd->bgqd/dot_general | solution.py:81
  235.7 8.1 %fusion.4 = f32[4,128]{1,0:T(4,128)S(1)} fusion(f32[1,4,128,8192]{3,2,1,0:T(8,128)} %get-tuple-element.44, f32[4,128]{1,0:T(4,128)S(1)} %max.19), kind=kLoop, calls=%fused_computation.11 | loop fusion | flops 8388096 | bytes 16781312 | tf_op jit(solution)/shard_map/reduce_sum | solution.py:78
  243.8 0.1 fusion.49
  243.9 1.0 fusion.38
  244.9 0.8 copy.128
  245.7 0.1 fusion.51
  245.7 0.2 fusion.40
  246.0 0.8 copy.129
  246.7 0.0 copy-done.1
  (17 shorter events, 0.1 us)
Async XLA Ops:
  0.6 32.0 %copy-start = (bf16[2048,512]{1,0:T(8,128)(2,1)S(1)}, bf16[2048,512]{1,0:T(8,128)(2,1)}, u32[]{:S(2)}) copy-start(bf16[2048,512]{1,0:T(8,128)(2,1)} %param.13) | copy-start | bytes 6291460
  49.0 27.5 %copy-start.3 = (bf16[128,4096]{1,0:T(8,128)(2,1)S(1)}, bf16[128,4096]{1,0:T(8,128)(2,1)}, u32[]{:S(2)}) copy-start(bf16[128,4096]{1,0:T(8,128)(2,1)} %param.10) | copy-start | bytes 3145732
  50.4 26.8 %copy-start.5 = (bf16[4096]{0:T(1024)(128)(2,1)S(1)}, bf16[4096]{0:T(1024)(128)(2,1)}, u32[]{:S(2)}) copy-start(bf16[4096]{0:T(1024)(128)(2,1)} %param.11) | copy-start | bytes 24580
  50.4 27.5 %copy-start.6 = (s32[1,32]{1,0:T(1,128)S(1)}, s32[1,32]{1,0:T(1,128)}, u32[]{:S(2)}) copy-start(s32[1,32]{1,0:T(1,128)} %param.15) | copy-start | bytes 388
  50.4 27.7 %copy-start.7 = (s32[128]{0:T(128)S(1)}, s32[128]{0:T(128)}, u32[]{:S(2)}) copy-start(s32[128]{0:T(128)} %param.19) | copy-start | bytes 1540
  69.9 99.5 %all-to-all-start = ((bf16[1,32,256,256]{3,2,0,1:T(8,128)(2,1)}), bf16[1,32,256,256]{3,2,0,1:T(8,128)(2,1)}, u32[]{:S(2)}, u32[]{:S(2)}) async-start(bf16[1,32,256,256]{3,2,0,1:T(8,128)(2,1)} %bitcast.168), calls=%async_computation | async-start | bytes 8388608 | tf_op jit(solution)/shard_map/all_to_all | solution.py:110
  91.7 84.6 %copy-start.4 = (f32[128,768]{0,1:T(8,128)}, f32[128,768]{0,1:T(8,128)S(1)}, u32[]{:S(2)}) copy-start(f32[128,768]{0,1:T(8,128)S(1)} %fusion.43) | copy-start | bytes 1179652
  209.8 8.9 %copy-start.2 = (bf16[8192,1,1,128]{0,3,2,1:T(8,128)(2,1)}, bf16[8192,1,1,128]{0,3,2,1:T(8,128)(2,1)S(1)}, u32[]{:S(2)}) copy-start(bf16[8192,1,1,128]{0,3,2,1:T(8,128)(2,1)S(1)} %copy.143) | copy-start | bytes 6291460
  227.5 19.2 %copy-start.1 = (bf16[2048,512]{1,0:T(8,128)(2,1)S(1)}, bf16[2048,512]{1,0:T(8,128)(2,1)}, u32[]{:S(2)}) copy-start(bf16[2048,512]{1,0:T(8,128)(2,1)} %param.13) | copy-start | bytes 6291460
